TPU v7x, 512 devices: a whole 4x4x16 slice. The times are simulated.
512 devices in a mesh: pipe: 8 (over y, x_lo), expert: 64 (over x_hi, z, core).
Axes of the slice: x: 4 (x_hi: 2, x_lo: 2; x = x_hi * 2 + x_lo), y: 4, z: 16, core: 2. Of those that a mesh axis runs over, the one named last changes fastest.
Arguments:
- fwd_tokens: bfloat16 [8, 1024, 3584], P('pipe', 'expert'), may hold values from -6 to 6
- fwd_routes: int32 [8, 1024, 2], P('pipe', 'expert'), may hold values from 0 to 7, all different within a row; in each aligned block of 16 rows (0 to 15, 16 to 31, ..., all dimensions but the last counted through in order) at most 6 rows name the same one
- fwd_scores: float32 [8, 1024, 2], P('pipe', 'expert'), may hold values from 0.1 to 1
- bwd_tokens: bfloat16 [8, 1024, 3584], P('pipe', 'expert'), may hold values from -6 to 6
- bwd_routes: int32 [8, 1024, 2], P('pipe', 'expert'), may hold values from 0 to 7, all different within a row; in each aligned block of 16 rows (0 to 15, 16 to 31, ..., all dimensions but the last counted through in order) at most 6 rows name the same one
- bwd_scores: float32 [8, 1024, 2], P('pipe', 'expert'), may hold values from 0.1 to 1
- out_grad: bfloat16 [8, 1024, 3584], P('pipe', 'expert'), may hold values from -6 to 6
- gate_weight: bfloat16 [8, 3584, 8192], P('pipe', None, 'expert'), may hold values from -0.09375 to 0.09375
- up_weight: bfloat16 [8, 3584, 8192], P('pipe', None, 'expert'), may hold values from -0.09375 to 0.09375
- down_weight: bfloat16 [8, 8192, 3584], P('pipe', 'expert'), may hold values from -0.1875 to 0.1875
Outputs:
- next_input: bfloat16 [8, 1024, 3584], P('pipe', 'expert')
- prev_grad: bfloat16 [8, 1024, 3584], P('pipe', 'expert')
Inputs may be any that keep to these rules, and one draw needn't show every extreme that they name: `fwd_routes`: each row names 2 different experts. Among the 16 rows of one device in one section, no expert is named more than 6 times, a bound that some block reaches. `bwd_routes`: each row names 2 different experts. Among the 16 rows of one device in one section, no expert is named more than 6 times, a bound that some block reaches.
All inputs are finite; a program needn't handle non-finite values.
Results may differ from a plain program's by a relative error of at most 0.011.
Values may be sent and summed in bfloat16 or wider, within the bound.
No kernel may reach another device: no remote copies, remote signals or barrier semaphores. Data moves between devices by JAX's collectives and lax.ppermute only.
A program may use at most 128 MiB of HBM per device.

v0:
```python
import jax
import jax.numpy as jnp
from jax import lax
from jax.sharding import PartitionSpec as P

GROUP = 8


def from_behind(value, axis, steps):
    count = lax.axis_size(axis)
    pairs = [(source, (source + steps) % count) for source in range(count)]
    return lax.ppermute(value, axis, pairs)


def route_tables(routes, scores, capacity, experts):
    tokens, topk = routes.shape
    flat = routes.reshape(-1)
    onehot = (flat[:, None] == jnp.arange(experts, dtype=jnp.int32)[None, :]).astype(jnp.int32)
    rank = jnp.cumsum(onehot, axis=0) - onehot
    within = jnp.sum(rank * onehot, axis=1)
    slot_ids = (flat * capacity + within).reshape(tokens, topk)
    places = jnp.arange(experts * capacity, dtype=jnp.int32)
    hits = (slot_ids[:, :, None] == places[None, None, :]).astype(jnp.float32)
    normed = scores / jnp.sum(scores, axis=1, keepdims=True)
    member = jnp.sum(hits, axis=1)
    weighted = jnp.sum(hits * normed[:, :, None], axis=1)
    return (member, weighted)


def pick_rows(member, rows):
    slots = jnp.einsum(
        "te,td->ed", member.astype(jnp.bfloat16), rows, preferred_element_type=jnp.float32
    )
    return slots.astype(jnp.bfloat16)


def expert_forward(rows3, w_gate, w_up, w_down):
    width = rows3.shape[-1]
    flat = rows3.reshape(-1, width)
    first = jnp.dot(flat, w_gate, preferred_element_type=jnp.float32)
    second = jnp.dot(flat, w_up, preferred_element_type=jnp.float32)
    hidden = (jax.nn.silu(first) * second).astype(jnp.bfloat16)
    parts = jnp.dot(hidden, w_down, preferred_element_type=jnp.float32).astype(jnp.bfloat16)
    return parts.reshape(rows3.shape)


def expert_backward(rows3, grads3, w_gate, w_up, w_down):
    width = rows3.shape[-1]
    flat = rows3.reshape(-1, width)
    first = jnp.dot(flat, w_gate, preferred_element_type=jnp.float32)
    second = jnp.dot(flat, w_up, preferred_element_type=jnp.float32)
    d_hidden = lax.dot_general(
        grads3.reshape(-1, width),
        w_down,
        (((1,), (1,)), ((), ())),
        preferred_element_type=jnp.float32,
    )
    sigm = 1.0 / (1.0 + jnp.exp(-first))
    d_first = (d_hidden * second * sigm * (1.0 + first * (1.0 - sigm))).astype(jnp.bfloat16)
    d_second = (d_hidden * first * sigm).astype(jnp.bfloat16)
    back = lax.dot_general(
        d_first, w_gate, (((1,), (1,)), ((), ())), preferred_element_type=jnp.float32
    )
    back = back + lax.dot_general(
        d_second, w_up, (((1,), (1,)), ((), ())), preferred_element_type=jnp.float32
    )
    return back.astype(jnp.bfloat16).reshape(rows3.shape)


def expert_work(arrived, weights):
    w_gate, w_up, w_down = weights
    kinds = arrived.shape[0]
    if kinds == 1:
        return expert_forward(arrived[0], w_gate, w_up, w_down)[None]
    return expert_backward(arrived[0], arrived[1], w_gate, w_up, w_down)[None]


def pass_rows(payload, weights):
    kinds, experts, capacity, width = payload.shape
    spread = jnp.broadcast_to(payload[:, :, None], (kinds, experts, GROUP, capacity, width))
    spread = spread.reshape(kinds, experts * GROUP, capacity, width)
    returned = lax.all_to_all(
        expert_work(
            lax.all_to_all(spread, "expert", split_axis=1, concat_axis=1, tiled=True), weights
        ),
        "expert",
        split_axis=1,
        concat_axis=1,
        tiled=True,
    )
    outkinds = returned.shape[0]
    summed = jnp.sum(
        returned.reshape(outkinds, experts, GROUP, capacity, width).astype(jnp.float32), axis=2
    )
    return summed.reshape(outkinds, experts * capacity, width)


def body(
    fwd_tokens,
    fwd_routes,
    fwd_scores,
    bwd_tokens,
    bwd_routes,
    bwd_scores,
    out_grad,
    gate_weight,
    up_weight,
    down_weight,
):
    experts = lax.axis_size("expert") // GROUP
    tokens = fwd_tokens.shape[1]
    topk = fwd_routes.shape[2]
    width = fwd_tokens.shape[2]
    capacity = min(tokens, max(6, (tokens * topk + experts - 1) // experts + 2))
    weights = (gate_weight[0], up_weight[0], down_weight[0])
    member_f, weight_f = route_tables(fwd_routes[0], fwd_scores[0], capacity, experts)
    member_b, weight_b = route_tables(bwd_routes[0], bwd_scores[0], capacity, experts)
    send_f = pick_rows(member_f, fwd_tokens[0]).reshape(experts, capacity, width)
    send_x = pick_rows(member_b, bwd_tokens[0]).reshape(experts, capacity, width)
    route_grad = jnp.einsum(
        "te,td->ed", weight_b, out_grad[0].astype(jnp.float32), precision=lax.Precision.HIGHEST
    )
    send_g = route_grad.astype(jnp.bfloat16).reshape(experts, capacity, width)
    sum_f = pass_rows(send_f[None], weights)[0]
    sum_b = pass_rows(jnp.stack((send_x, send_g)), weights)[0]
    layer_out = jnp.dot(weight_f, sum_f, precision=lax.Precision.HIGHEST).astype(jnp.bfloat16)[None]
    input_grad = jnp.dot(member_b, sum_b, precision=lax.Precision.HIGHEST).astype(jnp.bfloat16)[
        None
    ]
    next_input = from_behind(layer_out, "pipe", 1)
    prev_grad = from_behind(input_grad, "pipe", -1)
    return (next_input, prev_grad)


def solution(mesh):
    placed = (
        P("pipe", "expert", None),
        P("pipe", "expert", None),
        P("pipe", "expert", None),
        P("pipe", "expert", None),
        P("pipe", "expert", None),
        P("pipe", "expert", None),
        P("pipe", "expert", None),
        P("pipe", None, "expert"),
        P("pipe", None, "expert"),
        P("pipe", "expert", None),
    )
    return jax.shard_map(
        body,
        mesh=mesh,
        in_specs=placed,
        out_specs=(P("pipe", "expert", None), P("pipe", "expert", None)),
        check_vma=False,
    )
```

profile of v0, /device:TPU:30, one launch (start us, length us, event | category | flops | bytes accessed | tf_op | source)
XLA Modules:
  0.0 810.3 jit_solution(13249150855847399699)
XLA Ops:
  0.6 0.0 copy-start
  0.6 0.8 copy.39
  1.5 0.1 eq.56
  1.6 0.1 fusion.36
  1.6 0.1 reduce_window_sum.17
  1.7 0.2 select_reduce_fusion.3
  1.9 0.1 reduce_sum.95
  2.0 0.1 copy.40
  2.1 0.7 bitcast_add_fusion.1
  2.8 0.7 reduce_sum.96
  3.5 0.7 bitcast_divide_fusion.1
  4.1 0.1 convert_reduce_fusion.3
  4.2 1.2 convolution_convert_fusion.3
  5.4 0.1 broadcast_in_dim.12
  5.5 2.1 broadcast_in_dim.13
  7.6 19.0 %all-to-all-start = ((bf16[1,64,6,3584]{3,2,0,1:T(8,128)(2,1)}), bf16[1,64,6,3584]{3,2,0,1:T(8,128)(2,1)}, u32[]{:S(2)}, u32[]{:S(2)}) async-start(bf16[1,64,6,3584]{3,2,0,1:T(8,128)(2,1)} %bitcast.66), calls=%async_computation | async-start | bytes 7340032 | tf_op jit(solution)/shard_map/all_to_all | solution.py:84
  26.7 0.1 copy.42
  26.7 0.1 eq.63
  26.8 0.1 fusion.35
  26.9 0.1 reduce_window_sum.18
  27.0 0.2 select_reduce_fusion.1
  27.1 0.1 reduce_sum.101
  27.2 0.1 copy.43
  27.4 0.1 select_reduce_fusion
  27.5 0.0 copy-done.4
  27.5 0.3 convolution_convert_fusion.2
  27.7 0.1 stack_reshape.6
  27.9 0.5 convolution_convert_fusion.1
  28.4 0.1 stack_reshape.7
  28.5 0.2 pad_maximum_fusion
  28.7 0.7 copy.44
  29.4 161.7 %all-to-all-done = bf16[1,64,6,3584]{3,2,0,1:T(8,128)(2,1)} async-done(((bf16[1,64,6,3584]{3,2,0,1:T(8,128)(2,1)}), bf16[1,64,6,3584]{3,2,0,1:T(8,128)(2,1)}, u32[]{:S(2)}, u32[]{:S(2)}) %all-to-all-start) | async-done | bytes 2752544 | tf_op jit(solution)/shard_map/all_to_all | solution.py:84
  191.1 5.2 broadcast_in_dim.16
  196.3 9.4 %all-to-all-start.2 = ((bf16[2,64,6,3584]{3,0,2,1:T(2,128)(2,1)}), bf16[2,64,6,3584]{3,0,2,1:T(2,128)(2,1)}, u32[]{:S(2)}, u32[]{:S(2)}) async-start(bf16[2,64,6,3584]{3,0,2,1:T(2,128)(2,1)} %bitcast.63), calls=%async_computation.2 | async-start | bytes 11010048 | tf_op jit(solution)/shard_map/all_to_all | solution.py:84
  205.8 0.0 copy-start.2
  205.8 5.6 reshape_squeeze.11
  211.3 2.7 fusion.19
  214.1 6.3 convolution_convert_fusion
  220.4 5.4 broadcast_in_dim_reshape.8
  225.8 224.4 %all-to-all-done.2 = bf16[2,64,6,3584]{3,0,2,1:T(2,128)(2,1)} async-done(((bf16[2,64,6,3584]{3,0,2,1:T(2,128)(2,1)}), bf16[2,64,6,3584]{3,0,2,1:T(2,128)(2,1)}, u32[]{:S(2)}, u32[]{:S(2)}) %all-to-all-start.2) | async-done | bytes 5505056 | tf_op jit(solution)/shard_map/all_to_all | solution.py:84
  450.2 8.1 all-to-all-start.1
  458.4 37.1 %slice_reduce_fusion = (bf16[64,6,3584]{2,1,0:T(8,128)(2,1)}, bf16[64,6,3584]{2,1,0:T(8,128)(2,1)}) fusion(bf16[2,64,6,3584]{3,0,2,1:T(2,128)(2,1)} %all-to-all-done.2), kind=kLoop, calls=%fused_computation.5 | loop fusion | bytes 11010048 | tf_op jit(solution)/shard_map/slice | solution.py:75
  495.4 5.5 reshape_squeeze.13
  500.9 5.4 reshape_squeeze.12
  506.4 2.8 fusion.17
  509.2 0.9 fusion.8
  510.1 7.3 fusion.7
  517.3 5.0 fusion
  522.3 5.5 broadcast_in_dim_reshape.9
  527.8 95.1 %all-to-all-done.1 = bf16[1,64,6,3584]{3,2,0,1:T(8,128)(2,1)} async-done(((bf16[1,64,6,3584]{3,2,0,1:T(8,128)(2,1)}), bf16[1,64,6,3584]{3,2,0,1:T(8,128)(2,1)}, u32[]{:S(2)}, u32[]{:S(2)}) %all-to-all-start.1) | async-done | bytes 2752544 | tf_op jit(solution)/shard_map/all_to_all | solution.py:82
  622.8 9.4 %all-to-all-start.3 = ((bf16[1,64,6,3584]{3,2,0,1:T(8,128)(2,1)}), bf16[1,64,6,3584]{3,2,0,1:T(8,128)(2,1)}, u32[]{:S(2)}, u32[]{:S(2)}) async-start(bf16[1,64,6,3584]{3,2,0,1:T(8,128)(2,1)} %bitcast.65), calls=%async_computation.3 | async-start | bytes 7340032 | tf_op jit(solution)/shard_map/all_to_all | solution.py:82
  632.3 2.9 convert_reduce_fusion.1
  635.2 0.1 squeeze_reshape.6
  635.3 0.4 fusion.1
  635.7 2.4 collective-permute-start
  638.1 158.7 %all-to-all-done.3 = bf16[1,64,6,3584]{3,2,0,1:T(8,128)(2,1)} async-done(((bf16[1,64,6,3584]{3,2,0,1:T(8,128)(2,1)}), bf16[1,64,6,3584]{3,2,0,1:T(8,128)(2,1)}, u32[]{:S(2)}, u32[]{:S(2)}) %all-to-all-start.3) | async-done | bytes 2752544 | tf_op jit(solution)/shard_map/all_to_all | solution.py:82
  796.8 2.9 convert_reduce_fusion
  799.6 0.1 squeeze_reshape.7
  799.7 0.4 fusion.2
  800.2 2.7 collective-permute-start.1
  802.9 0.0 collective-permute-done
  803.0 6.0 collective-permute-done.1
  809.0 0.6 copy.50
  809.6 0.6 copy.51
  (16 shorter events, 0.1 us)
Async XLA Ops:
  0.6 213.5 %copy-start = (bf16[1,3584,128]{2,1,0:T(8,128)(2,1)S(1)}, bf16[1,3584,128]{2,1,0:T(8,128)(2,1)}, u32[]{:S(2)}) copy-start(bf16[1,3584,128]{2,1,0:T(8,128)(2,1)} %param.18) | copy-start | bytes 2752516
  7.6 19.0 %copy-start.6 = (s32[1,16,2]{1,2,0:T(2,128)S(1)}, s32[1,16,2]{1,2,0:T(2,128)}, u32[]{:S(2)}) copy-start(s32[1,16,2]{1,2,0:T(2,128)} %param.14) | copy-start | bytes 388
  7.6 19.7 %copy-start.7 = (f32[1,16,2]{1,2,0:T(2,128)S(1)}, f32[1,16,2]{1,2,0:T(2,128)}, u32[]{:S(2)}) copy-start(f32[1,16,2]{1,2,0:T(2,128)} %param.15) | copy-start | bytes 388
  7.6 19.8 %copy-start.4 = (bf16[1,16,3584]{2,1,0:T(8,128)(2,1)S(1)}, bf16[1,16,3584]{2,1,0:T(8,128)(2,1)}, u32[]{:S(2)}) copy-start(bf16[1,16,3584]{2,1,0:T(8,128)(2,1)} %param.13) | copy-start | bytes 344068
  7.6 20.3 %copy-start.5 = (bf16[1,16,3584]{2,1,0:T(8,128)(2,1)S(1)}, bf16[1,16,3584]{2,1,0:T(8,128)(2,1)}, u32[]{:S(2)}) copy-start(bf16[1,16,3584]{2,1,0:T(8,128)(2,1)} %param.16) | copy-start | bytes 344068
  7.6 183.5 %all-to-all-start = ((bf16[1,64,6,3584]{3,2,0,1:T(8,128)(2,1)}), bf16[1,64,6,3584]{3,2,0,1:T(8,128)(2,1)}, u32[]{:S(2)}, u32[]{:S(2)}) async-start(bf16[1,64,6,3584]{3,2,0,1:T(8,128)(2,1)} %bitcast.66), calls=%async_computation | async-start | bytes 7340032 | tf_op jit(solution)/shard_map/all_to_all | solution.py:84
  196.3 253.9 %all-to-all-start.2 = ((bf16[2,64,6,3584]{3,0,2,1:T(2,128)(2,1)}), bf16[2,64,6,3584]{3,0,2,1:T(2,128)(2,1)}, u32[]{:S(2)}, u32[]{:S(2)}) async-start(bf16[2,64,6,3584]{3,0,2,1:T(2,128)(2,1)} %bitcast.63), calls=%async_computation.2 | async-start | bytes 11010048 | tf_op jit(solution)/shard_map/all_to_all | solution.py:84
  205.8 5.6 copy-start.2
  211.3 2.7 copy-start.3
  450.2 172.6 %all-to-all-start.1 = ((bf16[1,64,6,3584]{3,2,0,1:T(8,128)(2,1)}), bf16[1,64,6,3584]{3,2,0,1:T(8,128)(2,1)}, u32[]{:S(2)}, u32[]{:S(2)}) async-start(bf16[1,64,6,3584]{3,2,0,1:T(8,128)(2,1)} %bitcast.64), calls=%async_computation.1 | async-start | bytes 7340032 | tf_op jit(solution)/shard_map/all_to_all | solution.py:82
  506.4 2.8 copy-start.1
  622.8 173.9 %all-to-all-start.3 = ((bf16[1,64,6,3584]{3,2,0,1:T(8,128)(2,1)}), bf16[1,64,6,3584]{3,2,0,1:T(8,128)(2,1)}, u32[]{:S(2)}, u32[]{:S(2)}) async-start(bf16[1,64,6,3584]{3,2,0,1:T(8,128)(2,1)} %bitcast.65), calls=%async_computation.3 | async-start | bytes 7340032 | tf_op jit(solution)/shard_map/all_to_all | solution.py:82
  635.7 167.2 %collective-permute-start = (bf16[1,16,3584]{2,1,0:T(8,128)(2,1)S(1)}, bf16[1,16,3584]{2,1,0:T(8,128)(2,1)S(1)}, u32[]{:S(2)}, u32[]{:S(2)}) collective-permute-start(bf16[1,16,3584]{2,1,0:T(8,128)(2,1)S(1)} %fusion.1), channel_id=1, source_target_pairs={{0,64},{64,128},{128,192},{192,256},{256,320},{320,384},{384,448},... | collective-permute-start | bytes 344072 | tf_op jit(solution)/shard_map/ppermute | solution.py:12
  800.2 8.8 %collective-permute-start.1 = (bf16[1,16,3584]{2,1,0:T(8,128)(2,1)S(1)}, bf16[1,16,3584]{2,1,0:T(8,128)(2,1)S(1)}, u32[]{:S(2)}, u32[]{:S(2)}) collective-permute-start(bf16[1,16,3584]{2,1,0:T(8,128)(2,1)S(1)} %fusion.2), channel_id=1, source_target_pairs={{0,448},{64,0},{128,64},{192,128},{256,192},{320,256},{384,320},{4... | collective-permute-start | bytes 344072 | tf_op jit(solution)/shard_map/ppermute | solution.py:12
where the time goes:
time: 812 us; the launch traced here: 810 us
  waiting for transfers between devices  646 us (80%)
  local copies, waits for them, and re-layouts  75.8 us (9%)
  starting transfers between devices  51.2 us (6%)
  matrix products  27.7 us (3%)
  other arithmetic  8.81 us (1%)
    all_to_all x2, waiting for transfers between devices, pass_rows(): lax.all_to_all(spread, 'expert', split_axis=1, concat_axis=1, tiled=True)  386 us
    all_to_all x2, waiting for transfers between devices, pass_rows(): lax.all_to_all(expert_work(lax.all_to_all(spread, 'expert', split_axis=1,...  254 us
    slice x1, local copies, waits for them, and re-layouts, expert_work(): return expert_backward(arrived[0], arrived[1], w_gate, w_up, w_down)[None]  37.1 us
    all_to_all x2, starting transfers between devices, pass_rows(): lax.all_to_all(spread, 'expert', split_axis=1, concat_axis=1, tiled=True)  28.5 us
    all_to_all x2, starting transfers between devices, pass_rows(): lax.all_to_all(expert_work(lax.all_to_all(spread, 'expert', split_axis=1,...  17.5 us
  transfers between devices with their start and end apart: 6, of which 5 were waited for; matrix products, arithmetic and copies ran while one was open for 12% of the time, Pallas kernels for 0%

commit v1 on v0

--- a/solution.py
+++ b/solution.py
@@ -79,14 +79,19 @@
     kinds, experts, capacity, width = payload.shape
     spread = jnp.broadcast_to(payload[:, :, None], (kinds, experts, GROUP, capacity, width))
     spread = spread.reshape(kinds, experts * GROUP, capacity, width)
-    returned = lax.all_to_all(
+
+    def clear_joints_on(incoming_x):
+        return jnp.concatenate(
+            lax.all_to_all(
+                jnp.stack(jnp.split(incoming_x, lax.axis_size("expert"), axis=1)), "expert", 0, 0
+            ),
+            axis=1,
+        )
+
+    returned = clear_joints_on(
         expert_work(
             lax.all_to_all(spread, "expert", split_axis=1, concat_axis=1, tiled=True), weights
-        ),
-        "expert",
-        split_axis=1,
-        concat_axis=1,
-        tiled=True,
+        )
     )
     outkinds = returned.shape[0]
     summed = jnp.sum(

time: 812 us -> 823 us (1.014)
  waiting for transfers between devices: 646 us -> 460 us
  local copies, waits for them, and re-layouts: 75.8 us -> 260 us
    unnamed x20 -> x144, local copies, waits for them, and re-layouts: 2.25 us -> 184 us
    all_to_all x2, waiting for transfers between devices: 254 us -> 160 us  [clear_joints_on(): lax.all_to_all(jnp.stack(jnp.split(incoming_x, lax.axis_size('expert'), a...]
    all_to_all x2, waiting for transfers between devices: 386 us -> 294 us  [pass_rows(): lax.all_to_all(spread, 'expert', split_axis=1, concat_axis=1, tiled=True)]
  transfers between devices with their start and end apart: 6 -> 6, of which waited for: 5 -> 5; matrix products, arithmetic and copies ran while one was open for 12% -> 35% of each run, Pallas kernels for 0% -> 0%
where the time goes in v1:
time: 823 us; the launch traced here: 815 us
  waiting for transfers between devices  460 us (56%)
  local copies, waits for them, and re-layouts  260 us (32%)
  starting transfers between devices  56.1 us (7%)
  matrix products  29.4 us (4%)
  other arithmetic  8.81 us (1%)
    all_to_all x2, waiting for transfers between devices, pass_rows(): lax.all_to_all(spread, 'expert', split_axis=1, concat_axis=1, tiled=True)  294 us
    unnamed x144, local copies, waits for them, and re-layouts  184 us
    all_to_all x2, waiting for transfers between devices, clear_joints_on(): lax.all_to_all(jnp.stack(jnp.split(incoming_x, lax.axis_size('expert'), a...  160 us
    slice x1, local copies, waits for them, and re-layouts, expert_work(): return expert_backward(arrived[0], arrived[1], w_gate, w_up, w_down)[None]  37.1 us
    all_to_all x2, starting transfers between devices, pass_rows(): lax.all_to_all(spread, 'expert', split_axis=1, concat_axis=1, tiled=True)  28.5 us
    all_to_all x2, starting transfers between devices, clear_joints_on(): lax.all_to_all(jnp.stack(jnp.split(incoming_x, lax.axis_size('expert'), a...  22.5 us
  transfers between devices with their start and end apart: 6, of which 5 were waited for; matrix products, arithmetic and copies ran while one was open for 35% of the time, Pallas kernels for 0%

profile of v1, /device:TPU:30, one launch (start us, length us, event | category | flops | bytes accessed | tf_op | source)
XLA Modules:
  0.0 815.2 jit_solution(1730408528768611244)
XLA Ops:
  5.5 2.1 broadcast_in_dim.13
  7.6 19.0 %all-to-all-start = ((bf16[1,64,6,3584]{3,2,0,1:T(8,128)(2,1)}), bf16[1,64,6,3584]{3,2,0,1:T(8,128)(2,1)}, u32[]{:S(2)}, u32[]{:S(2)}) async-start(bf16[1,64,6,3584]{3,2,0,1:T(8,128)(2,1)} %bitcast.574), calls=%async_computation | async-start | bytes 7340032 | tf_op jit(solution)/shard_map/all_to_all | solution.py:93
  29.4 161.7 %all-to-all-done = bf16[1,64,6,3584]{3,2,0,1:T(8,128)(2,1)} async-done(((bf16[1,64,6,3584]{3,2,0,1:T(8,128)(2,1)}), bf16[1,64,6,3584]{3,2,0,1:T(8,128)(2,1)}, u32[]{:S(2)}, u32[]{:S(2)}) %all-to-all-start) | async-done | bytes 2752544 | tf_op jit(solution)/shard_map/all_to_all | solution.py:93
  191.1 5.2 broadcast_in_dim.16
  196.3 9.4 %all-to-all-start.2 = ((bf16[2,64,6,3584]{3,0,2,1:T(2,128)(2,1)}), bf16[2,64,6,3584]{3,0,2,1:T(2,128)(2,1)}, u32[]{:S(2)}, u32[]{:S(2)}) async-start(bf16[2,64,6,3584]{3,0,2,1:T(2,128)(2,1)} %bitcast.573), calls=%async_computation.2 | async-start | bytes 11010048 | tf_op jit(solution)/shard_map/all_to_all | solution.py:93
  205.8 5.6 reshape_squeeze.11
  211.3 2.7 fusion.19
  214.1 6.4 convolution_convert_fusion
  220.5 5.4 broadcast_in_dim_reshape.8
  228.7 1.4 constant_dynamic-update-slice_fusion.61
  231.6 1.4 constant_dynamic-update-slice_fusion.59
  238.8 1.4 constant_dynamic-update-slice_fusion.54
  243.1 1.4 constant_dynamic-update-slice_fusion.51
  246.0 1.5 constant_dynamic-update-slice_fusion.49
  250.4 1.5 constant_dynamic-update-slice_fusion.46
  257.6 1.4 constant_dynamic-update-slice_fusion.41
  263.4 1.5 constant_dynamic-update-slice_fusion.37
  269.1 1.4 constant_dynamic-update-slice_fusion.33
  274.9 1.5 constant_dynamic-update-slice_fusion.29
  279.2 1.5 constant_dynamic-update-slice_fusion.26
  280.7 1.4 constant_dynamic-update-slice_fusion.25
  285.0 1.4 constant_dynamic-update-slice_fusion.22
  286.4 1.4 constant_dynamic-update-slice_fusion.21
  289.3 1.4 constant_dynamic-update-slice_fusion.19
  290.8 1.4 constant_dynamic-update-slice_fusion.18
  296.5 1.5 constant_dynamic-update-slice_fusion.14
  303.8 1.5 constant_dynamic-update-slice_fusion.9
  308.1 1.4 constant_dynamic-update-slice_fusion.6
  312.4 1.4 constant_dynamic-update-slice_fusion.3
  315.3 1.5 constant_dynamic-update-slice_fusion.1
  318.2 132.0 %all-to-all-done.2 = bf16[2,64,6,3584]{3,0,2,1:T(2,128)(2,1)} async-done(((bf16[2,64,6,3584]{3,0,2,1:T(2,128)(2,1)}), bf16[2,64,6,3584]{3,0,2,1:T(2,128)(2,1)}, u32[]{:S(2)}, u32[]{:S(2)}) %all-to-all-start.2) | async-done | bytes 5505056 | tf_op jit(solution)/shard_map/all_to_all | solution.py:93
  450.2 8.3 %all-to-all-start.1 = ((bf16[64,1,1,6,3584]{4,3,2,1,0:T(8,128)(2,1)}), bf16[64,1,1,6,3584]{4,3,2,1,0:T(8,128)(2,1)}, u32[]{:S(2)}, u32[]{:S(2)}) async-start(bf16[64,1,1,6,3584]{4,3,2,1,0:T(8,128)(2,1)} %constant_dynamic-update-slice_fusion), calls=%async_computation.1 | async-start | bytes 7340032 | tf_op jit(solution)/shard_map/all_to_all | solution.py:85
  458.5 37.1 %slice_reduce_fusion = (bf16[64,6,3584]{2,1,0:T(8,128)(2,1)}, bf16[64,6,3584]{2,1,0:T(8,128)(2,1)}) fusion(bf16[2,64,6,3584]{3,0,2,1:T(2,128)(2,1)} %all-to-all-done.2), kind=kLoop, calls=%fused_computation.5 | loop fusion | bytes 11010048 | tf_op jit(solution)/shard_map/slice | solution.py:75
  495.6 5.5 reshape_squeeze.13
  501.1 2.6 fusion.17
  503.8 5.5 reshape_squeeze.12
  509.2 2.6 fusion.8
  511.9 7.3 fusion.7
  519.1 5.0 fusion
  524.1 5.4 broadcast_in_dim_reshape.9
  532.5 1.4 constant_dynamic-update-slice_fusion.125
  538.2 1.5 constant_dynamic-update-slice_fusion.121
  544.0 1.4 constant_dynamic-update-slice_fusion.117
  548.3 1.5 constant_dynamic-update-slice_fusion.114
  557.0 1.5 constant_dynamic-update-slice_fusion.108
  561.3 1.5 constant_dynamic-update-slice_fusion.105
  565.6 1.4 constant_dynamic-update-slice_fusion.102
  571.4 1.4 constant_dynamic-update-slice_fusion.98
  572.9 1.4 constant_dynamic-update-slice_fusion.97
  577.2 1.5 constant_dynamic-update-slice_fusion.94
  578.6 1.4 constant_dynamic-update-slice_fusion.93
  588.7 1.4 constant_dynamic-update-slice_fusion.86
  593.0 1.4 constant_dynamic-update-slice_fusion.83
  601.7 1.5 constant_dynamic-update-slice_fusion.77
  603.1 1.5 constant_dynamic-update-slice_fusion.76
  611.8 1.4 constant_dynamic-update-slice_fusion.70
  617.5 1.5 constant_dynamic-update-slice_fusion.66
  623.0 14.2 %all-to-all-start.3 = ((bf16[64,1,1,6,3584]{4,3,2,1,0:T(8,128)(2,1)}), bf16[64,1,1,6,3584]{4,3,2,1,0:T(8,128)(2,1)}, u32[]{:S(2)}, u32[]{:S(2)}) async-start(bf16[64,1,1,6,3584]{4,3,2,1,0:T(8,128)(2,1)} %constant_dynamic-update-slice_fusion.64), calls=%async_computation.3 | async-start | bytes 7340032 | tf_op jit(solution)/shard_map/all_to_all | solution.py:85
  637.2 2.9 convert_reduce_fusion.1
  640.6 2.4 collective-permute-start
  643.1 158.6 %all-to-all-done.3 = bf16[64,1,1,6,3584]{4,3,2,1,0:T(8,128)(2,1)} async-done(((bf16[64,1,1,6,3584]{4,3,2,1,0:T(8,128)(2,1)}), bf16[64,1,1,6,3584]{4,3,2,1,0:T(8,128)(2,1)}, u32[]{:S(2)}, u32[]{:S(2)}) %all-to-all-start.3) | async-done | bytes 2752544 | tf_op jit(solution)/shard_map/all_to_all | solution.py:85
  801.7 2.9 convert_reduce_fusion
  805.1 2.7 collective-permute-start.1
  807.9 6.0 collective-permute-done.1
  (142 shorter events, 140.6 us)
Async XLA Ops:
  0.6 213.5 %copy-start = (bf16[1,3584,128]{2,1,0:T(8,128)(2,1)S(1)}, bf16[1,3584,128]{2,1,0:T(8,128)(2,1)}, u32[]{:S(2)}) copy-start(bf16[1,3584,128]{2,1,0:T(8,128)(2,1)} %param.18) | copy-start | bytes 2752516
  7.6 19.0 %copy-start.5 = (s32[1,16,2]{1,2,0:T(2,128)S(1)}, s32[1,16,2]{1,2,0:T(2,128)}, u32[]{:S(2)}) copy-start(s32[1,16,2]{1,2,0:T(2,128)} %param.14) | copy-start | bytes 388
  7.6 19.7 %copy-start.6 = (f32[1,16,2]{1,2,0:T(2,128)S(1)}, f32[1,16,2]{1,2,0:T(2,128)}, u32[]{:S(2)}) copy-start(f32[1,16,2]{1,2,0:T(2,128)} %param.15) | copy-start | bytes 388
  7.6 19.8 %copy-start.3 = (bf16[1,16,3584]{2,1,0:T(8,128)(2,1)S(1)}, bf16[1,16,3584]{2,1,0:T(8,128)(2,1)}, u32[]{:S(2)}) copy-start(bf16[1,16,3584]{2,1,0:T(8,128)(2,1)} %param.13) | copy-start | bytes 344068
  7.6 20.3 %copy-start.4 = (bf16[1,16,3584]{2,1,0:T(8,128)(2,1)S(1)}, bf16[1,16,3584]{2,1,0:T(8,128)(2,1)}, u32[]{:S(2)}) copy-start(bf16[1,16,3584]{2,1,0:T(8,128)(2,1)} %param.16) | copy-start | bytes 344068
  7.6 183.5 %all-to-all-start = ((bf16[1,64,6,3584]{3,2,0,1:T(8,128)(2,1)}), bf16[1,64,6,3584]{3,2,0,1:T(8,128)(2,1)}, u32[]{:S(2)}, u32[]{:S(2)}) async-start(bf16[1,64,6,3584]{3,2,0,1:T(8,128)(2,1)} %bitcast.574), calls=%async_computation | async-start | bytes 7340032 | tf_op jit(solution)/shard_map/all_to_all | solution.py:93
  196.3 253.9 %all-to-all-start.2 = ((bf16[2,64,6,3584]{3,0,2,1:T(2,128)(2,1)}), bf16[2,64,6,3584]{3,0,2,1:T(2,128)(2,1)}, u32[]{:S(2)}, u32[]{:S(2)}) async-start(bf16[2,64,6,3584]{3,0,2,1:T(2,128)(2,1)} %bitcast.573), calls=%async_computation.2 | async-start | bytes 11010048 | tf_op jit(solution)/shard_map/all_to_all | solution.py:93
  205.8 5.6 copy-start.1
  211.3 2.7 copy-start.2
  450.2 172.8 %all-to-all-start.1 = ((bf16[64,1,1,6,3584]{4,3,2,1,0:T(8,128)(2,1)}), bf16[64,1,1,6,3584]{4,3,2,1,0:T(8,128)(2,1)}, u32[]{:S(2)}, u32[]{:S(2)}) async-start(bf16[64,1,1,6,3584]{4,3,2,1,0:T(8,128)(2,1)} %constant_dynamic-update-slice_fusion), calls=%async_computation.1 | async-start | bytes 7340032 | tf_op jit(solution)/shard_map/all_to_all | solution.py:85
  623.0 178.7 %all-to-all-start.3 = ((bf16[64,1,1,6,3584]{4,3,2,1,0:T(8,128)(2,1)}), bf16[64,1,1,6,3584]{4,3,2,1,0:T(8,128)(2,1)}, u32[]{:S(2)}, u32[]{:S(2)}) async-start(bf16[64,1,1,6,3584]{4,3,2,1,0:T(8,128)(2,1)} %constant_dynamic-update-slice_fusion.64), calls=%async_computation.3 | async-start | bytes 7340032 | tf_op jit(solution)/shard_map/all_to_all | solution.py:85
  640.6 167.2 %collective-permute-start = (bf16[1,16,3584]{2,1,0:T(8,128)(2,1)S(1)}, bf16[1,16,3584]{2,1,0:T(8,128)(2,1)S(1)}, u32[]{:S(2)}, u32[]{:S(2)}) collective-permute-start(bf16[1,16,3584]{2,1,0:T(8,128)(2,1)S(1)} %fusion.1), channel_id=1, source_target_pairs={{0,64},{64,128},{128,192},{192,256},{256,320},{320,384},{384,448},... | collective-permute-start | bytes 344072 | tf_op jit(solution)/shard_map/ppermute | solution.py:12
  805.1 8.8 %collective-permute-start.1 = (bf16[1,16,3584]{2,1,0:T(8,128)(2,1)S(1)}, bf16[1,16,3584]{2,1,0:T(8,128)(2,1)S(1)}, u32[]{:S(2)}, u32[]{:S(2)}) collective-permute-start(bf16[1,16,3584]{2,1,0:T(8,128)(2,1)S(1)} %fusion.2), channel_id=1, source_target_pairs={{0,448},{64,0},{128,64},{192,128},{256,192},{320,256},{384,320},{4... | collective-permute-start | bytes 344072 | tf_op jit(solution)/shard_map/ppermute | solution.py:12
